TPU v7x, 256 devices: a whole 4x4x8 slice. The times are simulated.
256 devices in a mesh: dp: 16 (over y_lo, x, core), tensor: 16 (over z, y_hi).
Axes of the slice: x: 4, y: 4 (y_hi: 2, y_lo: 2; y = y_hi * 2 + y_lo), z: 8, core: 2. Of those that a mesh axis runs over, the one named last changes fastest.
Arguments:
- gate_pre: bfloat16 [8192, 14336], P('dp', 'tensor'), may hold values from -6 to 6
- up_pre: bfloat16 [8192, 14336], P('dp', 'tensor'), may hold values from -6 to 6
- grad_out: bfloat16 [8192, 4096], P(('dp', 'tensor')), may hold values from -24 to 24
- codes: bfloat16 [14336, 4096], P('tensor'), as said below
- scales: int32 [448, 4096], P('tensor'), may hold values from 117 to 120
Outputs:
- out: bfloat16 [8192, 4096], P(('dp', 'tensor'))
- grad_gate: bfloat16 [8192, 14336], P('dp', 'tensor')
- grad_up: bfloat16 [8192, 14336], P('dp', 'tensor')
- grad_weight: bfloat16 [14336, 4096], P('tensor', 'dp')
Inputs may be any that keep to these rules, and one draw needn't show every extreme that they name: `codes`: every entry is an FP8 E4M3 normal value (sign, exponent field 4 to 9, three mantissa bits), held exactly.
All inputs are finite; a program needn't handle non-finite values.
Results may differ from a plain program's by a relative error of at most 0.022.
Values may be sent and summed in bfloat16 or wider, within the bound.
No kernel may reach another device: no remote copies, remote signals or barrier semaphores. Data moves between devices by JAX's collectives and lax.ppermute only.
A program may use at most 128 MiB of HBM per device.

v0:
```python
import jax
import jax.numpy as jnp
from jax import lax
from jax.sharding import PartitionSpec as P


def decode(codes, scales):
    factor = jnp.exp2(scales.astype(jnp.float32) - 127.0).astype(jnp.bfloat16)
    blocks = codes.reshape(scales.shape[0], 32, codes.shape[1]) * factor[:, None, :]
    return blocks.reshape(codes.shape)


def weight_gradient(hidden, cotangent):
    partial_grad = lax.dot_general(
        hidden, cotangent, (((0,), (0,)), ((), ())), preferred_element_type=jnp.float32
    )
    return lax.psum_scatter(
        partial_grad.astype(jnp.bfloat16), "dp", scatter_dimension=1, tiled=True
    )


def per_device(gate_pre, up_pre, grad_out, codes, scales):
    weight = decode(codes, scales)
    gate_value = gate_pre.astype(jnp.float32)
    up_value = up_pre.astype(jnp.float32)
    sigmoid_gate = jax.nn.sigmoid(gate_value)
    hidden = (gate_value * sigmoid_gate * up_value).astype(jnp.bfloat16)
    out = lax.psum_scatter(
        jnp.dot(hidden, weight, preferred_element_type=jnp.float32).astype(jnp.bfloat16),
        "tensor",
        scatter_dimension=0,
        tiled=True,
    )
    cotangent = lax.all_gather(grad_out, "tensor", axis=0, tiled=True)
    grad_hidden = lax.dot_general(
        cotangent, weight, (((1,), (1,)), ((), ())), preferred_element_type=jnp.float32
    )
    grad_weight = weight_gradient(hidden, cotangent)
    grad_gate = (
        grad_hidden * up_value * sigmoid_gate * (1.0 + gate_value * (1.0 - sigmoid_gate))
    ).astype(jnp.bfloat16)
    grad_up = (grad_hidden * gate_value * sigmoid_gate).astype(jnp.bfloat16)
    return (out, grad_gate, grad_up, grad_weight)


def solution(mesh):
    in_specs = (
        P("dp", "tensor"),
        P("dp", "tensor"),
        P(("dp", "tensor"), None),
        P("tensor", None),
        P("tensor", None),
    )
    out_specs = (P(("dp", "tensor"), None), P("dp", "tensor"), P("dp", "tensor"), P("tensor", "dp"))
    return jax.shard_map(
        per_device, mesh=mesh, in_specs=in_specs, out_specs=out_specs, check_vma=False
    )
```

profile of v0, /device:TPU:16, one launch (start us, length us, event | category | flops | bytes accessed | tf_op | source)
XLA Modules:
  0.0 412.0 jit_solution(5260447283789857836)
XLA Ops:
  7.2 0.0 copy-start.1
  7.2 0.0 all-gather.2.cloned.1.call-start
  7.2 0.7 all-gather.2.cloned.1.call-update
  7.9 0.0 copy-start.4
  7.9 0.0 reduce-scatter.3.cloned.1.call-start
  8.0 2.3 copy.10
  10.2 0.0 copy-done.1
  10.2 1.3 copy.9
  11.5 0.0 copy-done.4
  11.5 0.1 exponential_convert_fusion
  11.6 3.7 bitcast_multiply_fusion
  15.3 0.0 copy-start
  15.3 2.9 copy-done
  18.2 8.0 %convolution_convert_fusion.1 = bf16[512,4096]{1,0:T(8,128)(2,1)} fusion(bf16[896,4096]{1,0:T(8,128)(2,1)S(1)} %bitcast_multiply_fusion, bf16[512,896]{0,1:T(8,128)(2,1)} %copy.10, bf16[512,896]{0,1:T(8,128)(2,1)} %copy.9), kind=kOutput, calls=%fused_computation.2 | convolution fusion | flops 3763863552 | bytes 13369344 | tf_op jit(solution)/shard_map/dot_general | solution.py:29
  26.3 0.0 copy-start.2
  26.3 0.0 copy-start.3
  26.3 0.0 reduce-scatter.3.cloned.1.call-update
  26.3 0.0 reduce-scatter.5.cloned.1.call-start
  26.3 84.5 %all-gather.2.cloned.1.call-done = bf16[512,4096]{1,0:T(8,128)(2,1)} async-done(((bf16[32,4096]{1,0:T(8,128)(2,1)}), bf16[512,4096]{1,0:T(8,128)(2,1)}) %all-gather.2.cloned.1.call-update) | async-done | bytes 4194320 | tf_op jit(solution)/shard_map/all_gather | solution.py:34
  110.9 0.0 copy-done.2
  110.9 0.0 copy-done.3
  110.9 8.4 %convolution_convert_fusion = bf16[896,4096]{1,0:T(8,128)(2,1)} fusion(bf16[512,4096]{1,0:T(8,128)(2,1)} %all-gather.2.cloned.1.call-done, bf16[512,896]{0,1:T(8,128)(2,1)S(1)} %copy-done.2, bf16[512,896]{0,1:T(8,128)(2,1)S(1)} %copy-done.3), kind=kOutput, calls=%fused_computation.1 | convolution fusion | flops 3765436416 | bytes 13369344 | tf_op jit(solution)/shard_map/dot_general | solution.py:14
  119.3 0.0 reduce-scatter.5.cloned.1.call-update
  119.3 9.8 %fusion.9 = (bf16[512,896]{0,1:T(8,128)(2,1)S(1)}, bf16[512,896]{0,1:T(8,128)(2,1)}) fusion(bf16[512,896]{0,1:T(8,128)(2,1)S(1)} %copy-done.3, bf16[512,896]{0,1:T(8,128)(2,1)S(1)} %copy-done.2, bf16[896,4096]{1,0:T(8,128)(2,1)} %copy-done, bf16[512,4096]{1,0:T(8,128)(2,1)} %all-gather.2.cloned.1.call-done), kind=kOutput, calls=%fused_computation.18 | convolution fusion | flops 3764977664 | bytes 15204352 | tf_op jit(solution)/shard_map/dot_general | solution.py:35
  129.1 2.2 copy.11
  131.3 1.3 copy.12
  132.6 194.3 %reduce-scatter.3.cloned.1.call-done = bf16[32,4096]{1,0:T(8,128)(2,1)} async-done(((bf16[512,4096]{1,0:T(8,128)(2,1)}), bf16[32,4096]{1,0:T(8,128)(2,1)}) %reduce-scatter.3.cloned.1.call-update) | async-done | bytes 262160 | tf_op jit(solution)/shard_map/reduce_scatter | solution.py:28
  326.9 78.5 %reduce-scatter.5.cloned.1.call-done = bf16[896,256]{1,0:T(8,128)(2,1)} async-done(((bf16[896,4096]{1,0:T(8,128)(2,1)}), bf16[896,256]{1,0:T(8,128)(2,1)}) %reduce-scatter.5.cloned.1.call-update) | async-done | bytes 458768 | tf_op jit(solution)/shard_map/reduce_scatter | solution.py:17
Async XLA Ops:
  7.2 3.1 copy-start.1
  7.2 103.7 %all-gather.2.cloned.1.call-start = ((), (), s32[]{:S(2)}) async-start(), calls=%async_computation.3 | async-start | bytes 4456448 | tf_op jit(solution)/shard_map/all_gather | solution.py:34
  7.9 3.6 copy-start.4
  7.9 319.0 %reduce-scatter.3.cloned.1.call-start = ((), (), s32[]{:S(2)}) async-start(), calls=%async_computation.2 | async-start | bytes 4456448 | tf_op jit(solution)/shard_map/reduce_scatter | solution.py:28
  15.3 2.9 copy-start
  26.3 84.6 %copy-start.2 = (bf16[512,896]{0,1:T(8,128)(2,1)S(1)}, bf16[512,896]{0,1:T(8,128)(2,1)}, u32[]{:S(2)}) copy-start(bf16[512,896]{0,1:T(8,128)(2,1)} %copy.10) | copy-start | bytes 2752516
  26.3 84.6 %copy-start.3 = (bf16[512,896]{0,1:T(8,128)(2,1)S(1)}, bf16[512,896]{0,1:T(8,128)(2,1)}, u32[]{:S(2)}) copy-start(bf16[512,896]{0,1:T(8,128)(2,1)} %copy.9) | copy-start | bytes 2752516
  26.3 379.1 %reduce-scatter.5.cloned.1.call-start = ((), (), s32[]{:S(2)}) async-start(), calls=%async_computation.4 | async-start | bytes 7798784 | tf_op jit(solution)/shard_map/reduce_scatter | solution.py:17
Sparse Core Ops, SparseCore 0:
  10.6 100.2 all-gather.1
  115.5 211.3 reduce-scatter.2
  330.0 75.3 reduce-scatter.4
where the time goes:
time: 412 us
  waiting for transfers between devices  358 us (87%)
  matrix products  26.2 us (6%)
  between operations  13.8 us (3%)
  local copies, waits for them, and re-layouts  9.97 us (2%)
    reduce_scatter x1, waiting for transfers between devices, per_device(): lax.psum_scatter(jnp.dot(hidden, weight, preferred_element_type=jnp.float...  194 us
    all_gather x1, waiting for transfers between devices, per_device(): cotangent = lax.all_gather(grad_out, 'tensor', axis=0, tiled=True)  84.5 us
    reduce_scatter x1, waiting for transfers between devices, weight_gradient(): lax.psum_scatter(partial_grad.astype(jnp.bfloat16), 'dp', scatter_dimensi...  78.5 us
    unnamed x14, local copies, waits for them, and re-layouts  9.97 us
    dot_general x1, matrix products, per_device(): lax.dot_general(cotangent, weight, (((1,), (1,)), ((), ())), preferred_el...  9.8 us
    dot_general x1, matrix products, weight_gradient(): lax.dot_general(hidden, cotangent, (((0,), (0,)), ((), ())), preferred_el...  8.41 us
  transfers between devices with their start and end apart: 3, of which 3 were waited for; matrix products, arithmetic and copies ran while one was open for 9% of the time, Pallas kernels for 0%

commit v1 on v0

--- a/solution.py
+++ b/solution.py
@@ -31,7 +31,9 @@
         scatter_dimension=0,
         tiled=True,
     )
-    cotangent = lax.all_gather(grad_out, "tensor", axis=0, tiled=True)
+    cotangent = jnp.concatenate(
+        lax.all_to_all(jnp.stack([grad_out] * lax.axis_size("tensor")), "tensor", 0, 0), axis=0
+    )
     grad_hidden = lax.dot_general(
         cotangent, weight, (((1,), (1,)), ((), ())), preferred_element_type=jnp.float32
     )

time: 412 us -> 375 us (0.910)
  waiting for transfers between devices: 358 us -> 306 us
  starting transfers between devices: 0.12 us -> 11.7 us
    all_to_all x0 -> x1, waiting for transfers between devices: none -> 90.6 us  [per_device(): lax.all_to_all(jnp.stack([grad_out] * lax.axis_size('tensor')), 'tensor',...]
    all_gather x1 -> x0, waiting for transfers between devices: 84.5 us -> none  [per_device(): cotangent = lax.all_gather(grad_out, 'tensor', axis=0, tiled=True)]
    reduce_scatter x1, waiting for transfers between devices: 194 us -> 137 us  [per_device(): lax.psum_scatter(jnp.dot(hidden, weight, preferred_element_type=jnp.float...]
    all_to_all x0 -> x1, starting transfers between devices: none -> 11.6 us  [per_device(): lax.all_to_all(jnp.stack([grad_out] * lax.axis_size('tensor')), 'tensor',...]
    unnamed x14 -> x16, local copies, waits for them, and re-layouts: 9.97 us -> 9 us
  transfers between devices with their start and end apart: 3 -> 3, of which waited for: 3 -> 3; matrix products, arithmetic and copies ran while one was open for 9% -> 10% of each run, Pallas kernels for 0% -> 0%
where the time goes in v1:
time: 375 us; the launch traced here: 374 us
  waiting for transfers between devices  306 us (82%)
  matrix products  26.3 us (7%)
  between operations  14.1 us (4%)
  local copies, waits for them, and re-layouts  12.5 us (3%)
  starting transfers between devices  11.7 us (3%)
  other arithmetic  3.78 us (1%)
    reduce_scatter x1, waiting for transfers between devices, per_device(): lax.psum_scatter(jnp.dot(hidden, weight, preferred_element_type=jnp.float...  137 us
    all_to_all x1, waiting for transfers between devices, per_device(): lax.all_to_all(jnp.stack([grad_out] * lax.axis_size('tensor')), 'tensor',...  90.6 us
    reduce_scatter x1, waiting for transfers between devices, weight_gradient(): lax.psum_scatter(partial_grad.astype(jnp.bfloat16), 'dp', scatter_dimensi...  78.5 us
    all_to_all x1, starting transfers between devices, per_device(): lax.all_to_all(jnp.stack([grad_out] * lax.axis_size('tensor')), 'tensor',...  11.6 us
    dot_general x1, matrix products, per_device(): lax.dot_general(cotangent, weight, (((1,), (1,)), ((), ())), preferred_el...  9.88 us
    unnamed x16, local copies, waits for them, and re-layouts  9 us
    dot_general x1, matrix products, weight_gradient(): lax.dot_general(hidden, cotangent, (((0,), (0,)), ((), ())), preferred_el...  8.45 us
    dot_general x1, matrix products, per_device(): jnp.dot(hidden, weight, preferred_element_type=jnp.float32)  8.01 us
  transfers between devices with their start and end apart: 3, of which 3 were waited for; matrix products, arithmetic and copies ran while one was open for 10% of the time, Pallas kernels for 0%

profile of v1, /device:TPU:16, one launch (start us, length us, event | category | flops | bytes accessed | tf_op | source)
XLA Modules:
  0.0 374.4 jit_solution(15893544604850621305)
XLA Ops:
  7.2 3.5 stack.2
  10.7 0.0 copy-start.5
  10.7 0.0 copy-start.1
  10.7 11.6 %all-to-all-start = ((bf16[16,32,4096]{2,1,0:T(8,128)(2,1)}), bf16[16,32,4096]{2,1,0:T(8,128)(2,1)}, u32[]{:S(2)}, u32[]{:S(2)}) async-start(bf16[16,32,4096]{2,1,0:T(8,128)(2,1)} %stack.2), calls=%async_computation.1 | async-start | bytes 8388608 | tf_op jit(solution)/shard_map/all_to_all | solution.py:35
  22.3 0.0 copy-start.2
  22.3 0.0 reduce-scatter.3.cloned.1.call-start
  22.3 0.0 copy-done.5
  22.3 0.1 exponential_convert_fusion
  22.5 0.0 copy-done.1
  22.5 1.3 copy.10
  23.8 0.0 copy-done.2
  23.8 1.3 copy.9
  25.0 3.7 bitcast_multiply_fusion
  28.7 0.0 copy-start
  28.7 2.9 copy-done
  31.7 8.0 %convolution_convert_fusion.1 = bf16[512,4096]{1,0:T(8,128)(2,1)} fusion(bf16[896,4096]{1,0:T(8,128)(2,1)S(1)} %bitcast_multiply_fusion, bf16[512,896]{0,1:T(8,128)(2,1)} %copy.10, bf16[512,896]{0,1:T(8,128)(2,1)} %copy.9), kind=kOutput, calls=%fused_computation.2 | convolution fusion | flops 3763863552 | bytes 13369344 | tf_op jit(solution)/shard_map/dot_general | solution.py:29
  39.7 0.0 copy-start.3
  39.7 0.0 copy-start.4
  39.7 0.0 reduce-scatter.3.cloned.1.call-update
  39.7 0.0 reduce-scatter.5.cloned.1.call-start
  39.7 90.6 %all-to-all-done = bf16[16,32,4096]{2,1,0:T(8,128)(2,1)} async-done(((bf16[16,32,4096]{2,1,0:T(8,128)(2,1)}), bf16[16,32,4096]{2,1,0:T(8,128)(2,1)}, u32[]{:S(2)}, u32[]{:S(2)}) %all-to-all-start) | async-done | bytes 4194336 | tf_op jit(solution)/shard_map/all_to_all | solution.py:35
  130.4 0.0 copy-done.3
  130.4 0.0 copy-done.4
  130.4 8.4 %convolution_convert_fusion = bf16[896,4096]{1,0:T(8,128)(2,1)} fusion(bf16[512,4096]{1,0:T(8,128)(2,1)} %bitcast.1, bf16[512,896]{0,1:T(8,128)(2,1)S(1)} %copy-done.3, bf16[512,896]{0,1:T(8,128)(2,1)S(1)} %copy-done.4), kind=kOutput, calls=%fused_computation.1 | convolution fusion | flops 3765436416 | bytes 13369344 | tf_op jit(solution)/shard_map/dot_general | solution.py:14
  138.8 0.0 reduce-scatter.5.cloned.1.call-update
  138.8 9.9 %fusion.9 = (bf16[512,896]{0,1:T(8,128)(2,1)S(1)}, bf16[512,896]{0,1:T(8,128)(2,1)}) fusion(bf16[512,896]{0,1:T(8,128)(2,1)S(1)} %copy-done.4, bf16[512,896]{0,1:T(8,128)(2,1)S(1)} %copy-done.3, bf16[896,4096]{1,0:T(8,128)(2,1)} %copy-done, bf16[512,4096]{1,0:T(8,128)(2,1)} %bitcast.1), kind=kOutput, calls=%fused_computation.18 | convolution fusion | flops 3764977664 | bytes 15204352 | tf_op jit(solution)/shard_map/dot_general | solution.py:37
  148.7 2.2 copy.11
  150.9 1.3 copy.12
  152.2 136.8 %reduce-scatter.3.cloned.1.call-done = bf16[32,4096]{1,0:T(8,128)(2,1)} async-done(((bf16[512,4096]{1,0:T(8,128)(2,1)}), bf16[32,4096]{1,0:T(8,128)(2,1)}) %reduce-scatter.3.cloned.1.call-update) | async-done | bytes 262160 | tf_op jit(solution)/shard_map/reduce_scatter | solution.py:28
  289.1 78.5 %reduce-scatter.5.cloned.1.call-done = bf16[896,256]{1,0:T(8,128)(2,1)} async-done(((bf16[896,4096]{1,0:T(8,128)(2,1)}), bf16[896,256]{1,0:T(8,128)(2,1)}) %reduce-scatter.5.cloned.1.call-update) | async-done | bytes 458768 | tf_op jit(solution)/shard_map/reduce_scatter | solution.py:17
Async XLA Ops:
  10.7 11.6 %copy-start.5 = (s32[28,4096]{1,0:T(8,128)S(1)}, s32[28,4096]{1,0:T(8,128)}, u32[]{:S(2)}) copy-start(s32[28,4096]{1,0:T(8,128)} %param.9) | copy-start | bytes 1376260
  10.7 11.8 %copy-start.1 = (bf16[512,896]{1,0:T(8,128)(2,1)S(1)}, bf16[512,896]{1,0:T(8,128)(2,1)}, u32[]{:S(2)}) copy-start(bf16[512,896]{1,0:T(8,128)(2,1)} %param.6) | copy-start | bytes 2752516
  10.7 119.7 %all-to-all-start = ((bf16[16,32,4096]{2,1,0:T(8,128)(2,1)}), bf16[16,32,4096]{2,1,0:T(8,128)(2,1)}, u32[]{:S(2)}, u32[]{:S(2)}) async-start(bf16[16,32,4096]{2,1,0:T(8,128)(2,1)} %stack.2), calls=%async_computation.1 | async-start | bytes 8388608 | tf_op jit(solution)/shard_map/all_to_all | solution.py:35
  22.3 1.5 copy-start.2
  22.3 266.8 %reduce-scatter.3.cloned.1.call-start = ((), (), s32[]{:S(2)}) async-start(), calls=%async_computation.3 | async-start | bytes 4456448 | tf_op jit(solution)/shard_map/reduce_scatter | solution.py:28
  28.7 2.9 copy-start
  39.7 90.7 %copy-start.3 = (bf16[512,896]{0,1:T(8,128)(2,1)S(1)}, bf16[512,896]{0,1:T(8,128)(2,1)}, u32[]{:S(2)}) copy-start(bf16[512,896]{0,1:T(8,128)(2,1)} %copy.10) | copy-start | bytes 2752516
  39.7 90.7 %copy-start.4 = (bf16[512,896]{0,1:T(8,128)(2,1)S(1)}, bf16[512,896]{0,1:T(8,128)(2,1)}, u32[]{:S(2)}) copy-start(bf16[512,896]{0,1:T(8,128)(2,1)} %copy.9) | copy-start | bytes 2752516
  39.7 327.8 %reduce-scatter.5.cloned.1.call-start = ((), (), s32[]{:S(2)}) async-start(), calls=%async_computation.4 | async-start | bytes 7798784 | tf_op jit(solution)/shard_map/reduce_scatter | solution.py:17
Sparse Core Ops, SparseCore 0:
  39.8 249.1 reduce-scatter.2
  292.2 75.2 reduce-scatter.4
